TPU v7x, 128 devices: a whole 4x4x4 slice. The times are simulated.
128 devices in a mesh: req: 16 (over y, z), mp: 8 (over x, core).
Axes of the slice: x: 4, y: 4, z: 4, core: 2. Of those that a mesh axis runs over, the one named last changes fastest.
Arguments:
- hidden_in: bfloat16 [16384, 2048], P('req', 'mp'), may hold values from -6 to 6
- w_qkv: bfloat16 [3, 2048, 2048], P(None, 'req', 'mp'), may hold values from -0.125 to 0.125
- w_out: bfloat16 [2048, 2048], P('mp', 'req'), may hold values from -0.125 to 0.125
- attn_gain: bfloat16 [2048], replicated, may hold values from 0.099609375 to 1.8984375
- mlp_gain: bfloat16 [2048], replicated, may hold values from 0.099609375 to 1.8984375
- w_gate: bfloat16 [2048, 8192], P('req', 'mp'), may hold values from -0.125 to 0.125
- w_up: bfloat16 [2048, 8192], P('req', 'mp'), may hold values from -0.125 to 0.125
- w_down: bfloat16 [8192, 2048], P('mp', 'req'), may hold values from -0.0625 to 0.0625
- k_cache: bfloat16 [16, 4096, 2048], P('req', None, 'mp'), may hold values from -363 to 363
- v_cache: bfloat16 [16, 4096, 2048], P('req', None, 'mp'), may hold values from -6 to 6
- cache_len: int32 [16], P('req'), may hold values from 256 to 4096, as said below
Outputs:
- hidden_out: bfloat16 [16384, 2048], P('req', 'mp')
- new_keys: bfloat16 [16384, 2048], P('req', 'mp')
- new_values: bfloat16 [16384, 2048], P('req', 'mp')
Inputs may be any that keep to these rules, and one draw needn't show every extreme that they name: Each request uses its first cache_len slots; later slots hold unused data. Some request's cache is full in every draw.
All inputs are finite; a program needn't handle non-finite values.
Results may differ from a plain program's by a relative error of at most 0.02.
Values may be sent and summed in bfloat16 or wider, within the bound.
No kernel may reach another device: no remote copies, remote signals or barrier semaphores. Data moves between devices by JAX's collectives and lax.ppermute only.
A program may use at most 128 MiB of HBM per device.

v0:
```python
import jax
import jax.numpy as jnp
from jax import lax
from jax.sharding import PartitionSpec as P

HD = 64
THETA = 130000.0
EPSILON = 1e-05
NEG_FILL = -1e30


def rms_scale(rows, gain):
    values = rows.astype(jnp.float32)
    meansq = jnp.mean(values * values, axis=-1, keepdims=True)
    return (values * lax.rsqrt(meansq + EPSILON) * gain.astype(jnp.float32)).astype(jnp.bfloat16)


def rotate(tensor, positions):
    half = tensor.shape[-1] // 2
    freq = THETA ** (-(jnp.arange(half, dtype=jnp.float32) * 2.0 / tensor.shape[-1]))
    angle = positions[:, None, None] * freq[None, None, :]
    cosine = jnp.cos(angle)
    sine = jnp.sin(angle)
    first = tensor[..., :half]
    second = tensor[..., half:]
    return jnp.concatenate(
        [first * cosine - second * sine, second * cosine + first * sine], axis=-1
    )


def absorb(carry, queries, keys, values, valid):
    top, total, accum = carry
    scores = jnp.einsum("qhd,khd->hqk", queries, keys, preferred_element_type=jnp.float32) * HD ** (
        -0.5
    )
    scores = jnp.where(valid[None], scores, NEG_FILL)
    new_top = jnp.maximum(top, jnp.max(scores, axis=-1, keepdims=True))
    factor = jnp.exp(top - new_top)
    probs = jnp.where(valid[None], jnp.exp(scores - new_top), 0.0)
    total = total * factor + jnp.sum(probs, axis=-1, keepdims=True)
    accum = accum * factor + jnp.einsum(
        "hqk,khd->hqd", probs.astype(jnp.bfloat16), values, preferred_element_type=jnp.float32
    )
    return (new_top, total, accum)


def on_device(
    hidden_in, w_qkv, w_out, attn_gain, mlp_gain, w_gate, w_up, w_down, k_cache, v_cache, cache_len
):
    new_count = hidden_in.shape[0]
    width = w_qkv.shape[2]
    heads_local = width // HD
    slots = k_cache.shape[1]
    full_rows = lax.all_gather(hidden_in, "mp", axis=1, tiled=True)
    normed = rms_scale(full_rows, attn_gain)
    columns = normed
    projected = jnp.einsum(
        "nd,kdw->knw",
        columns,
        lax.all_gather(w_qkv, "req", axis=1, tiled=True),
        preferred_element_type=jnp.float32,
    )
    length = cache_len[0]
    positions = (length + jnp.arange(new_count, dtype=jnp.int32)).astype(jnp.float32)
    queries = rotate(projected[0].reshape(new_count, heads_local, HD), positions).astype(
        jnp.bfloat16
    )
    fresh_keys = rotate(projected[1].reshape(new_count, heads_local, HD), positions).astype(
        jnp.bfloat16
    )
    fresh_values = projected[2].astype(jnp.bfloat16).reshape(new_count, heads_local, HD)
    rows = jnp.arange(new_count, dtype=jnp.int32)
    causal = rows[:, None] >= rows[None, :]
    start_carry = (
        jnp.full((heads_local, new_count, 1), NEG_FILL, jnp.float32),
        jnp.zeros((heads_local, new_count, 1), jnp.float32),
        jnp.zeros((heads_local, new_count, HD), jnp.float32),
    )
    carry = absorb(start_carry, queries, fresh_keys, fresh_values, causal)
    cache_keys = k_cache[0].reshape(slots, heads_local, HD)
    cache_values = v_cache[0].reshape(slots, heads_local, HD)
    block = min(slots, 512)
    count = (length + block - 1) // block

    def step_block(index, state):
        begin = index * block
        keys = lax.dynamic_slice_in_dim(cache_keys, begin, block, 0)
        values = lax.dynamic_slice_in_dim(cache_values, begin, block, 0)
        valid = (begin + jnp.arange(block, dtype=jnp.int32) < length)[None, :]
        return absorb(state, queries, keys, values, valid)

    top, total, accum = lax.fori_loop(0, count, step_block, carry)
    attn = (accum / total).transpose(1, 0, 2).reshape(new_count, width).astype(jnp.bfloat16)
    partial_value = jnp.dot(
        attn, lax.all_gather(w_out, "req", axis=1, tiled=True), preferred_element_type=jnp.float32
    )
    summed = lax.psum_scatter(
        partial_value.astype(jnp.bfloat16), "mp", scatter_dimension=1, tiled=True
    ).astype(jnp.float32)
    mid_local = (hidden_in.astype(jnp.float32) + summed).astype(jnp.bfloat16)
    mid_full = lax.all_gather(mid_local, "mp", axis=1, tiled=True)
    normed2 = rms_scale(mid_full, mlp_gain)
    columns = normed2
    gate = jnp.dot(
        columns,
        lax.all_gather(w_gate, "req", axis=0, tiled=True),
        preferred_element_type=jnp.float32,
    )
    upper = jnp.dot(
        columns, lax.all_gather(w_up, "req", axis=0, tiled=True), preferred_element_type=jnp.float32
    )
    units = (jax.nn.silu(gate) * upper).astype(jnp.bfloat16)
    terms = jnp.dot(
        units, lax.all_gather(w_down, "req", axis=1, tiled=True), preferred_element_type=jnp.float32
    )
    reduced = lax.psum_scatter(
        terms.astype(jnp.bfloat16), "mp", scatter_dimension=1, tiled=True
    ).astype(jnp.float32)
    hidden_out = (mid_local.astype(jnp.float32) + reduced).astype(jnp.bfloat16)
    return (
        hidden_out,
        fresh_keys.reshape(new_count, width),
        fresh_values.reshape(new_count, width),
    )


def solution(mesh):
    return jax.shard_map(
        on_device,
        mesh=mesh,
        in_specs=(
            P("req", "mp"),
            P(None, "req", "mp"),
            P("mp", "req"),
            P(),
            P(),
            P("req", "mp"),
            P("req", "mp"),
            P("mp", "req"),
            P("req", None, "mp"),
            P("req", None, "mp"),
            P("req"),
        ),
        out_specs=(P("req", "mp"), P("req", "mp"), P("req", "mp")),
        check_vma=False,
    )
```

profile of v0, /device:TPU:0, one launch (start us, length us, event | category | flops | bytes accessed | tf_op | source)
XLA Modules:
  0.0 499.0 jit_solution(9587442802145398446)
XLA Ops:
  7.9 1.7 copy.15
  10.5 1.3 iota_compare_fusion
  13.1 2.9 copy.17
  16.1 4.2 copy.18
  20.8 27.4 %all-gather.8.cloned.1.call-done = bf16[1024,2048]{1,0:T(8,128)(2,1)} async-done(((bf16[1024,256]{1,0:T(8,128)(2,1)}), bf16[1024,2048]{1,0:T(8,128)(2,1)}) %all-gather.8.cloned.1.call-update) | async-done | bytes 4194320 | tf_op jit(solution)/shard_map/all_gather | solution.py:54
  48.2 3.1 fusion.23
  51.3 53.4 %all-gather.10.cloned.1.call-done = bf16[3,2048,256]{1,2,0:T(8,128)(2,1)} async-done(((bf16[3,128,256]{1,2,0:T(8,128)(2,1)}), bf16[3,2048,256]{1,2,0:T(8,128)(2,1)}) %all-gather.10.cloned.1.call-update) | async-done | bytes 3145744 | tf_op jit(solution)/shard_map/all_gather | solution.py:60
  104.7 6.6 %fusion.37 = f32[3,1024,256]{1,2,0:T(8,128)S(1)} fusion(bf16[3,2048,256]{1,2,0:T(8,128)(2,1)} %all-gather.10.cloned.1.call-done, bf16[1024,2048]{1,0:T(8,128)(2,1)} %all-gather.8.cloned.1.call-done, f32[2048]{0:T(1024)S(1)} %convert_element_type.87, f32[1024]{0:T(1024)S(1)} %add_rsqrt_fusion.1), kind=kOutput, calls=%fused_computation.49 | convolution fusion | flops 3229614080 | bytes 10498048 | tf_op jit(solution)/shard_map/nd,kdw->knw/dot_general | solution.py:57
  113.3 3.0 fusion.20
  116.4 4.2 fusion.22
  120.6 5.9 %fusion.40 = f32[4,1024,64]{1,2,0:T(8,128)} fusion(bf16[1024,4,64]{0,2,1:T(8,128)(2,1)S(1)} %bitcast.80, f32[4,1024,1024]{1,2,0:T(8,128)S(1)} %get-tuple-element.91, f32[4,1024]{1,0:T(4,128)S(1)} %get-tuple-element.87, pred[1024,1024]{0,1:T(8,128)(4,1)S(1)} %copy-done.1, f32[4,1024]{1,0:T(4,128)S(1)} %get-tuple-element.85), kind=kOutput, calls=%fused_computation.50 | convolution fusion | flops 558104576 | bytes 19431424 | tf_op jit(solution)/shard_map/hqk,khd->hqd/dot_general | solution.py:41
  126.5 8.1 %while.14 = (s32[]{:T(128)}, f32[4,1024,1]{1,0,2:T(4,128)S(1)}, f32[4,1024,1]{1,0,2:T(4,128)S(1)}, f32[4,1024,64]{1,2,0:T(8,128)}, s32[]{:T(128)}, /*index=5*/s3...) while((s32[]{:T(128)}, f32[4,1024,1]{1,0,2:T(4,128)S(1)}, ...), condition=%wide.region_6.7_spmd, body=%wide.region_3.6_spmd.sunk | while | flops 564671488 | bytes 36965104 | solution.py:92
  127.3 1.6 bitcast_reduce_fusion.2
  128.9 3.1 fusion.74
  132.0 2.5 fusion.73
  134.6 1.4 divide_convert_fusion
  136.0 13.5 %all-gather.12.cloned.1.call-done = bf16[256,2048]{1,0:T(8,128)(2,1)} async-done(((bf16[256,128]{1,0:T(8,128)(2,1)}), bf16[256,2048]{1,0:T(8,128)(2,1)}) %all-gather.12.cloned.1.call-update) | async-done | bytes 1048592 | tf_op jit(solution)/shard_map/all_gather | solution.py:95
  149.5 4.5 convolution_convert_fusion
  154.1 79.0 %reduce-scatter.3.cloned.1.call-done = bf16[1024,256]{1,0:T(8,128)(2,1)} async-done(((bf16[1024,2048]{1,0:T(8,128)(2,1)}), bf16[1024,256]{1,0:T(8,128)(2,1)}) %reduce-scatter.3.cloned.1.call-update) | async-done | bytes 524304 | tf_op jit(solution)/shard_map/reduce_scatter | solution.py:97
  233.1 2.0 add_convert_fusion.1
  237.5 32.8 %all-gather.14.cloned.1.call-done = bf16[1024,2048]{1,0:T(8,128)(2,1)} async-done(((bf16[1024,256]{1,0:T(8,128)(2,1)}), bf16[1024,2048]{1,0:T(8,128)(2,1)}) %all-gather.14.cloned.1.call-update) | async-done | bytes 4194320 | tf_op jit(solution)/shard_map/all_gather | solution.py:101
  270.3 3.1 fusion.26
  273.4 51.6 %all-gather.16.cloned.1.call-done = bf16[2048,1024]{1,0:T(8,128)(2,1)} async-done(((bf16[128,1024]{1,0:T(8,128)(2,1)}), bf16[2048,1024]{1,0:T(8,128)(2,1)}) %all-gather.16.cloned.1.call-update) | async-done | bytes 4194320 | tf_op jit(solution)/shard_map/all_gather | solution.py:106
  325.0 10.0 %fusion.44 = f32[1024,1024]{1,0:T(8,128)} fusion(bf16[2048,1024]{1,0:T(8,128)(2,1)} %all-gather.16.cloned.1.call-done, bf16[1024,2048]{1,0:T(8,128)(2,1)} %all-gather.14.cloned.1.call-done, f32[2048]{0:T(1024)S(1)} %convert_element_type.102, f32[1024]{0:T(1024)S(1)} %add_rsqrt_fusion), kind=kOutput, calls=%fused_computation.51 | convolution fusion | flops 4303355904 | bytes 12595200 | tf_op jit(solution)/shard_map/dot_general | solution.py:104
  335.0 43.5 %all-gather.18.cloned.1.call-done = bf16[2048,1024]{1,0:T(8,128)(2,1)} async-done(((bf16[128,1024]{1,0:T(8,128)(2,1)}), bf16[2048,1024]{1,0:T(8,128)(2,1)}) %all-gather.18.cloned.1.call-update) | async-done | bytes 4194320 | tf_op jit(solution)/shard_map/all_gather | solution.py:110
  378.4 59.4 %all-gather.20.cloned.1.call-done = bf16[1024,2048]{1,0:T(8,128)(2,1)} async-done(((bf16[1024,128]{1,0:T(8,128)(2,1)}), bf16[1024,2048]{1,0:T(8,128)(2,1)}) %all-gather.20.cloned.1.call-update) | async-done | bytes 4194320 | tf_op jit(solution)/shard_map/all_gather | solution.py:114
  437.9 15.4 %convolution_convert_fusion.1 = bf16[1024,2048]{1,0:T(8,128)(2,1)} fusion(bf16[1024,2048]{1,0:T(8,128)(2,1)} %all-gather.20.cloned.1.call-done, f32[1024,1024]{1,0:T(8,128)} %fusion.44, bf16[2048,1024]{1,0:T(8,128)(2,1)} %all-gather.18.cloned.1.call-done, bf16[1024,2048]{1,0:T(8,128)(2,1)} %all-gather.14.cloned.1.call-done, ...), kind=kOutput, calls=%fused_computation.48 | convolution fusion | flops 8606711808 | bytes 20983808 | tf_op jit(solution)/shard_map/dot_general | solution.py:113
  453.3 1.0 copy.19
  454.3 1.3 slice_bitcast_fusion
  455.6 1.0 copy.20
  456.6 33.9 %reduce-scatter.5.cloned.1.call-done = bf16[1024,256]{1,0:T(8,128)(2,1)} async-done(((bf16[1024,2048]{1,0:T(8,128)(2,1)}), bf16[1024,256]{1,0:T(8,128)(2,1)}) %reduce-scatter.5.cloned.1.call-update) | async-done | bytes 524304 | tf_op jit(solution)/shard_map/reduce_scatter | solution.py:116
  490.5 2.0 add_convert_fusion
  (51 shorter events, 8.0 us)
Async XLA Ops:
  7.2 41.0 %all-gather.8.cloned.1.call-start = ((), (), s32[]{:S(2)}) async-start(), calls=%async_computation.2 | async-start | bytes 4718592 | tf_op jit(solution)/shard_map/all_gather | solution.py:54
  7.9 96.8 %all-gather.10.cloned.1.call-start = ((), (), s32[]{:S(2)}) async-start(), calls=%async_computation.3 | async-start | bytes 3342336 | tf_op jit(solution)/shard_map/all_gather | solution.py:60
  9.7 139.8 %all-gather.12.cloned.1.call-start = ((), (), s32[]{:S(2)}) async-start(), calls=%async_computation.4 | async-start | bytes 1114112 | tf_op jit(solution)/shard_map/all_gather | solution.py:95
  10.4 222.7 %reduce-scatter.3.cloned.1.call-start = ((), (), s32[]{:S(2)}) async-start(), calls=%async_computation.5 | async-start | bytes 4718592 | tf_op jit(solution)/shard_map/reduce_scatter | solution.py:97
  111.3 1.7 copy-start.2
  111.3 2.0 copy-start.1
  126.5 2.4 copy-start.4
  132.0 2.6 copy-start.5
  134.6 98.5 %copy-start.3 = (bf16[1024,256]{1,0:T(8,128)(2,1)S(1)}, bf16[1024,256]{1,0:T(8,128)(2,1)}, u32[]{:S(2)}) copy-start(bf16[1024,256]{1,0:T(8,128)(2,1)} %param.13) | copy-start | bytes 1572868
  134.6 102.9 %copy-start.6 = (bf16[2048]{0:T(1024)(128)(2,1)S(1)}, bf16[2048]{0:T(1024)(128)(2,1)}, u32[]{:S(2)}) copy-start(bf16[2048]{0:T(1024)(128)(2,1)} %param.17) | copy-start | bytes 12292
  154.0 116.3 %all-gather.14.cloned.1.call-start = ((), (), s32[]{:S(2)}) async-start(), calls=%async_computation.6 | async-start | bytes 4718592 | tf_op jit(solution)/shard_map/all_gather | solution.py:101
  235.1 89.9 %all-gather.16.cloned.1.call-start = ((), (), s32[]{:S(2)}) async-start(), calls=%async_computation.7 | async-start | bytes 4456448 | tf_op jit(solution)/shard_map/all_gather | solution.py:106
  235.7 142.7 %all-gather.18.cloned.1.call-start = ((), (), s32[]{:S(2)}) async-start(), calls=%async_computation.8 | async-start | bytes 4456448 | tf_op jit(solution)/shard_map/all_gather | solution.py:110
  236.4 201.4 %all-gather.20.cloned.1.call-start = ((), (), s32[]{:S(2)}) async-start(), calls=%async_computation.9 | async-start | bytes 4456448 | tf_op jit(solution)/shard_map/all_gather | solution.py:114
  237.2 253.3 %reduce-scatter.5.cloned.1.call-start = ((), (), s32[]{:S(2)}) async-start(), calls=%async_computation.10 | async-start | bytes 4718592 | tf_op jit(solution)/shard_map/reduce_scatter | solution.py:116
  453.3 37.2 %copy-start = (bf16[1024,256]{1,0:T(8,128)(2,1)S(1)}, bf16[1024,256]{1,0:T(8,128)(2,1)}, u32[]{:S(2)}) copy-start(bf16[1024,256]{1,0:T(8,128)(2,1)} %add_convert_fusion.1) | copy-start | bytes 1572868
Sparse Core Ops, SparseCore 0:
  9.7 38.4 all-gather.7
  50.9 53.7 all-gather.9
  106.8 42.7 all-gather.11
  154.2 78.9 reduce-scatter.2
  235.2 35.0 all-gather.13
  272.3 52.6 all-gather.15
  327.2 51.2 all-gather.17
  380.5 57.2 all-gather.19
  453.4 37.0 reduce-scatter.4
where the time goes:
time: 500 us; the launch traced here: 499 us
  waiting for transfers between devices  398 us (80%)
  matrix products  50 us (10%)
  other arithmetic  21.9 us (4%)
  between operations  14.7 us (3%)
  local copies, waits for them, and re-layouts  13.8 us (3%)
    reduce_scatter x1, waiting for transfers between devices, on_device(): lax.psum_scatter(partial_value.astype(jnp.bfloat16), 'mp', scatter_dimens...  79 us
    all_gather x1, waiting for transfers between devices, on_device(): lax.all_gather(w_down, 'req', axis=1, tiled=True)  59.4 us
    all_gather x1, waiting for transfers between devices, on_device(): lax.all_gather(w_qkv, 'req', axis=1, tiled=True)  53.4 us
    all_gather x1, waiting for transfers between devices, on_device(): lax.all_gather(w_gate, 'req', axis=0, tiled=True)  51.6 us
    all_gather x1, waiting for transfers between devices, on_device(): lax.all_gather(w_up, 'req', axis=0, tiled=True)  43.5 us
    reduce_scatter x1, waiting for transfers between devices, on_device(): lax.psum_scatter(terms.astype(jnp.bfloat16), 'mp', scatter_dimension=1, t...  33.9 us
    all_gather x1, waiting for transfers between devices, on_device(): mid_full = lax.all_gather(mid_local, 'mp', axis=1, tiled=True)  32.8 us
    all_gather x1, waiting for transfers between devices, on_device(): full_rows = lax.all_gather(hidden_in, 'mp', axis=1, tiled=True)  27.4 us
  transfers between devices with their start and end apart: 9, of which 9 were waited for; matrix products, arithmetic and copies ran while one was open for 12% of the time, Pallas kernels for 0%

commit v1 on v0

--- a/solution.py
+++ b/solution.py
@@ -7,6 +7,11 @@
 THETA = 130000.0
 EPSILON = 1e-05
 NEG_FILL = -1e30
+
+
+def gather_from_all(x, axis, dim):
+    copies = jnp.concatenate([x] * lax.axis_size(axis), axis=dim)
+    return lax.all_to_all(copies, axis, dim, dim, tiled=True)
 
 
 def rms_scale(rows, gain):
@@ -101,11 +106,7 @@
     mid_full = lax.all_gather(mid_local, "mp", axis=1, tiled=True)
     normed2 = rms_scale(mid_full, mlp_gain)
     columns = normed2
-    gate = jnp.dot(
-        columns,
-        lax.all_gather(w_gate, "req", axis=0, tiled=True),
-        preferred_element_type=jnp.float32,
-    )
+    gate = jnp.dot(columns, gather_from_all(w_gate, "req", 0), preferred_element_type=jnp.float32)
     upper = jnp.dot(
         columns, lax.all_gather(w_up, "req", axis=0, tiled=True), preferred_element_type=jnp.float32
     )

time: 500 us -> 461 us (0.922)
  waiting for transfers between devices: 398 us -> 350 us
  starting transfers between devices: 0.57 us -> 7.68 us
    all_gather x1 -> x0, waiting for transfers between devices: 51.6 us -> none  [on_device(): lax.all_gather(w_gate, 'req', axis=0, tiled=True)]
    all_to_all x0 -> x1, waiting for transfers between devices: none -> 24.2 us  [gather_from_all(): return lax.all_to_all(copies, axis, dim, dim, tiled=True)]
    all_gather x1, waiting for transfers between devices: 43.5 us -> 32.6 us  [on_device(): lax.all_gather(w_up, 'req', axis=0, tiled=True)]
    all_gather x1, waiting for transfers between devices: 32.8 us -> 23.9 us  [on_device(): mid_full = lax.all_gather(mid_local, 'mp', axis=1, tiled=True)]
    all_to_all x0 -> x1, starting transfers between devices: none -> 7.14 us  [gather_from_all(): return lax.all_to_all(copies, axis, dim, dim, tiled=True)]
    unnamed x15 -> x34, local copies, waits for them, and re-layouts: 12.2 us -> 14.5 us
  transfers between devices with their start and end apart: 9 -> 9, of which waited for: 9 -> 9; matrix products, arithmetic and copies ran while one was open for 12% -> 13% of each run, Pallas kernels for 0% -> 0%
where the time goes in v1:
time: 461 us; the launch traced here: 460 us
  waiting for transfers between devices  350 us (76%)
  matrix products  50 us (11%)
  other arithmetic  21.8 us (5%)
  local copies, waits for them, and re-layouts  16 us (3%)
  between operations  15.1 us (3%)
  starting transfers between devices  7.68 us (2%)
    reduce_scatter x1, waiting for transfers between devices, on_device(): lax.psum_scatter(partial_value.astype(jnp.bfloat16), 'mp', scatter_dimens...  78.3 us
    all_gather x1, waiting for transfers between devices, on_device(): lax.all_gather(w_down, 'req', axis=1, tiled=True)  59.4 us
    all_gather x1, waiting for transfers between devices, on_device(): lax.all_gather(w_qkv, 'req', axis=1, tiled=True)  53.4 us
    reduce_scatter x1, waiting for transfers between devices, on_device(): lax.psum_scatter(terms.astype(jnp.bfloat16), 'mp', scatter_dimension=1, t...  33.9 us
    all_gather x1, waiting for transfers between devices, on_device(): lax.all_gather(w_up, 'req', axis=0, tiled=True)  32.6 us
    all_gather x1, waiting for transfers between devices, on_device(): full_rows = lax.all_gather(hidden_in, 'mp', axis=1, tiled=True)  27.4 us
    all_to_all x1, waiting for transfers between devices, gather_from_all(): return lax.all_to_all(copies, axis, dim, dim, tiled=True)  24.2 us
    all_gather x1, waiting for transfers between devices, on_device(): mid_full = lax.all_gather(mid_local, 'mp', axis=1, tiled=True)  23.9 us
  transfers between devices with their start and end apart: 9, of which 9 were waited for; matrix products, arithmetic and copies ran while one was open for 13% of the time, Pallas kernels for 0%

profile of v1, /device:TPU:0, one launch (start us, length us, event | category | flops | bytes accessed | tf_op | source)
XLA Modules:
  0.0 460.2 jit_solution(12348870092223546699)
XLA Ops:
  7.9 1.7 copy.15
  10.5 1.3 iota_compare_fusion
  13.2 2.9 copy.17
  16.1 4.1 copy.18
  20.8 27.4 %all-gather.7.cloned.1.call-done = bf16[1024,2048]{1,0:T(8,128)(2,1)} async-done(((bf16[1024,256]{1,0:T(8,128)(2,1)}), bf16[1024,2048]{1,0:T(8,128)(2,1)}) %all-gather.7.cloned.1.call-update) | async-done | bytes 4194320 | tf_op jit(solution)/shard_map/all_gather | solution.py:59
  48.2 3.1 fusion.23
  51.3 53.4 %all-gather.9.cloned.1.call-done = bf16[3,2048,256]{1,2,0:T(8,128)(2,1)} async-done(((bf16[3,128,256]{1,2,0:T(8,128)(2,1)}), bf16[3,2048,256]{1,2,0:T(8,128)(2,1)}) %all-gather.9.cloned.1.call-update) | async-done | bytes 3145744 | tf_op jit(solution)/shard_map/all_gather | solution.py:65
  104.7 6.6 %fusion.37 = f32[3,1024,256]{1,2,0:T(8,128)S(1)} fusion(bf16[3,2048,256]{1,2,0:T(8,128)(2,1)} %all-gather.9.cloned.1.call-done, bf16[1024,2048]{1,0:T(8,128)(2,1)} %all-gather.7.cloned.1.call-done, f32[2048]{0:T(1024)S(1)} %convert_element_type.87, f32[1024]{0:T(1024)S(1)} %add_rsqrt_fusion.1), kind=kOutput, calls=%fused_computation.49 | convolution fusion | flops 3229614080 | bytes 10498048 | tf_op jit(solution)/shard_map/nd,kdw->knw/dot_general | solution.py:62
  113.3 3.0 fusion.20
  116.4 4.2 fusion.22
  120.6 5.9 %fusion.40 = f32[4,1024,64]{1,2,0:T(8,128)} fusion(bf16[1024,4,64]{0,2,1:T(8,128)(2,1)S(1)} %bitcast.83, f32[4,1024,1024]{1,2,0:T(8,128)S(1)} %get-tuple-element.91, f32[4,1024]{1,0:T(4,128)S(1)} %get-tuple-element.87, pred[1024,1024]{0,1:T(8,128)(4,1)S(1)} %copy-done.3, f32[4,1024]{1,0:T(4,128)S(1)} %get-tuple-element.85), kind=kOutput, calls=%fused_computation.50 | convolution fusion | flops 558104576 | bytes 19431424 | tf_op jit(solution)/shard_map/hqk,khd->hqd/dot_general | solution.py:46
  126.5 8.0 %while.14 = (s32[]{:T(128)}, f32[4,1024,1]{1,0,2:T(4,128)S(1)}, f32[4,1024,1]{1,0,2:T(4,128)S(1)}, f32[4,1024,64]{1,2,0:T(8,128)}, s32[]{:T(128)}, /*index=5*/s3...) while((s32[]{:T(128)}, f32[4,1024,1]{1,0,2:T(4,128)S(1)}, ...), condition=%wide.region_6.7_spmd, body=%wide.region_3.6_spmd.sunk | while | flops 564671488 | bytes 36965104 | solution.py:97
  127.2 1.6 bitcast_reduce_fusion.2
  128.8 3.1 fusion.74
  131.9 2.5 fusion.73
  134.5 1.3 divide_convert_fusion
  135.8 13.7 %all-gather.11.cloned.1.call-done = bf16[256,2048]{1,0:T(8,128)(2,1)} async-done(((bf16[256,128]{1,0:T(8,128)(2,1)}), bf16[256,2048]{1,0:T(8,128)(2,1)}) %all-gather.11.cloned.1.call-update) | async-done | bytes 1048592 | tf_op jit(solution)/shard_map/all_gather | solution.py:100
  149.5 4.5 convolution_convert_fusion
  154.1 78.3 %reduce-scatter.3.cloned.1.call-done = bf16[1024,256]{1,0:T(8,128)(2,1)} async-done(((bf16[1024,2048]{1,0:T(8,128)(2,1)}), bf16[1024,256]{1,0:T(8,128)(2,1)}) %reduce-scatter.3.cloned.1.call-update) | async-done | bytes 524304 | tf_op jit(solution)/shard_map/reduce_scatter | solution.py:102
  232.5 2.0 add_convert_fusion.1
  236.2 1.9 copy-done.1
  238.2 7.1 %all-to-all-start = ((bf16[16,128,1024]{2,1,0:T(8,128)(2,1)}), bf16[16,128,1024]{2,1,0:T(8,128)(2,1)}, u32[]{:S(2)}, u32[]{:S(2)}) async-start(bf16[16,128,1024]{2,1,0:T(8,128)(2,1)} %bitcast.76), calls=%async_computation.1 | async-start | bytes 8388608 | tf_op jit(solution)/shard_map/all_to_all | solution.py:14
  245.6 23.9 %all-gather.13.cloned.1.call-done = bf16[1024,2048]{1,0:T(8,128)(2,1)} async-done(((bf16[1024,256]{1,0:T(8,128)(2,1)}), bf16[1024,2048]{1,0:T(8,128)(2,1)}) %all-gather.13.cloned.1.call-update) | async-done | bytes 4194320 | tf_op jit(solution)/shard_map/all_gather | solution.py:106
  269.5 3.1 fusion.26
  272.6 24.2 %all-to-all-done = bf16[16,128,1024]{2,1,0:T(8,128)(2,1)} async-done(((bf16[16,128,1024]{2,1,0:T(8,128)(2,1)}), bf16[16,128,1024]{2,1,0:T(8,128)(2,1)}, u32[]{:S(2)}, u32[]{:S(2)}) %all-to-all-start) | async-done | bytes 4194336 | tf_op jit(solution)/shard_map/all_to_all | solution.py:14
  296.8 9.9 %fusion.44 = f32[1024,1024]{1,0:T(8,128)} fusion(bf16[2048,1024]{1,0:T(8,128)(2,1)} %bitcast.19, bf16[1024,2048]{1,0:T(8,128)(2,1)} %all-gather.13.cloned.1.call-done, f32[2048]{0:T(1024)S(1)} %convert_element_type.102, f32[1024]{0:T(1024)S(1)} %add_rsqrt_fusion), kind=kOutput, calls=%fused_computation.51 | convolution fusion | flops 4303355904 | bytes 12595200 | tf_op jit(solution)/shard_map/dot_general | solution.py:109
  306.7 32.6 %all-gather.15.cloned.1.call-done = bf16[2048,1024]{1,0:T(8,128)(2,1)} async-done(((bf16[128,1024]{1,0:T(8,128)(2,1)}), bf16[2048,1024]{1,0:T(8,128)(2,1)}) %all-gather.15.cloned.1.call-update) | async-done | bytes 4194320 | tf_op jit(solution)/shard_map/all_gather | solution.py:111
  339.3 59.4 %all-gather.17.cloned.1.call-done = bf16[1024,2048]{1,0:T(8,128)(2,1)} async-done(((bf16[1024,128]{1,0:T(8,128)(2,1)}), bf16[1024,2048]{1,0:T(8,128)(2,1)}) %all-gather.17.cloned.1.call-update) | async-done | bytes 4194320 | tf_op jit(solution)/shard_map/all_gather | solution.py:115
  398.8 15.3 %convolution_convert_fusion.1 = bf16[1024,2048]{1,0:T(8,128)(2,1)} fusion(bf16[1024,2048]{1,0:T(8,128)(2,1)} %all-gather.17.cloned.1.call-done, f32[1024,1024]{1,0:T(8,128)} %fusion.44, bf16[2048,1024]{1,0:T(8,128)(2,1)} %all-gather.15.cloned.1.call-done, bf16[1024,2048]{1,0:T(8,128)(2,1)} %all-gather.13.cloned.1.call-done, ...), kind=kOutput, calls=%fused_computation.48 | convolution fusion | flops 8606711808 | bytes 20983808 | tf_op jit(solution)/shard_map/dot_general | solution.py:114
  415.2 1.3 slice_bitcast_fusion
  417.5 33.9 %reduce-scatter.5.cloned.1.call-done = bf16[1024,256]{1,0:T(8,128)(2,1)} async-done(((bf16[1024,2048]{1,0:T(8,128)(2,1)}), bf16[1024,256]{1,0:T(8,128)(2,1)}) %reduce-scatter.5.cloned.1.call-update) | async-done | bytes 524304 | tf_op jit(solution)/shard_map/reduce_scatter | solution.py:117
  451.4 2.0 add_convert_fusion
  (70 shorter events, 9.5 us)
Async XLA Ops:
  7.2 41.0 %all-gather.7.cloned.1.call-start = ((), (), s32[]{:S(2)}) async-start(), calls=%async_computation.3 | async-start | bytes 4718592 | tf_op jit(solution)/shard_map/all_gather | solution.py:59
  7.9 96.8 %all-gather.9.cloned.1.call-start = ((), (), s32[]{:S(2)}) async-start(), calls=%async_computation.4 | async-start | bytes 3342336 | tf_op jit(solution)/shard_map/all_gather | solution.py:65
  9.7 139.8 %all-gather.11.cloned.1.call-start = ((), (), s32[]{:S(2)}) async-start(), calls=%async_computation.5 | async-start | bytes 1114112 | tf_op jit(solution)/shard_map/all_gather | solution.py:100
  10.4 222.0 %reduce-scatter.3.cloned.1.call-start = ((), (), s32[]{:S(2)}) async-start(), calls=%async_computation.6 | async-start | bytes 4718592 | tf_op jit(solution)/shard_map/reduce_scatter | solution.py:102
  111.3 1.7 copy-start.4
  111.3 2.0 copy-start.3
  127.2 1.6 copy-start.6
  131.9 2.6 copy-start.7
  149.5 82.9 %copy-start.5 = (bf16[1024,256]{1,0:T(8,128)(2,1)S(1)}, bf16[1024,256]{1,0:T(8,128)(2,1)}, u32[]{:S(2)}) copy-start(bf16[1024,256]{1,0:T(8,128)(2,1)} %param.13) | copy-start | bytes 1572868
  154.1 81.7 %copy-start = (bf16[128,1024]{1,0:T(8,128)(2,1)S(1)}, bf16[128,1024]{1,0:T(8,128)(2,1)}, u32[]{:S(2)}) copy-start(bf16[128,1024]{1,0:T(8,128)(2,1)} %param.18) | copy-start | bytes 786436
  154.1 115.5 %all-gather.13.cloned.1.call-start = ((), (), s32[]{:S(2)}) async-start(), calls=%async_computation.7 | async-start | bytes 4718592 | tf_op jit(solution)/shard_map/all_gather | solution.py:106
  234.5 104.9 %all-gather.15.cloned.1.call-start = ((), (), s32[]{:S(2)}) async-start(), calls=%async_computation.8 | async-start | bytes 4456448 | tf_op jit(solution)/shard_map/all_gather | solution.py:111
  235.0 163.7 %all-gather.17.cloned.1.call-start = ((), (), s32[]{:S(2)}) async-start(), calls=%async_computation.9 | async-start | bytes 4456448 | tf_op jit(solution)/shard_map/all_gather | solution.py:115
  236.2 1.9 copy-start.1
  238.2 7.4 %copy-start.8 = (bf16[2048]{0:T(1024)(128)(2,1)S(1)}, bf16[2048]{0:T(1024)(128)(2,1)}, u32[]{:S(2)}) copy-start(bf16[2048]{0:T(1024)(128)(2,1)} %param.17) | copy-start | bytes 12292
  238.2 58.6 %all-to-all-start = ((bf16[16,128,1024]{2,1,0:T(8,128)(2,1)}), bf16[16,128,1024]{2,1,0:T(8,128)(2,1)}, u32[]{:S(2)}, u32[]{:S(2)}) async-start(bf16[16,128,1024]{2,1,0:T(8,128)(2,1)} %bitcast.76), calls=%async_computation.1 | async-start | bytes 8388608 | tf_op jit(solution)/shard_map/all_to_all | solution.py:14
  245.3 206.1 %reduce-scatter.5.cloned.1.call-start = ((), (), s32[]{:S(2)}) async-start(), calls=%async_computation.10 | async-start | bytes 4718592 | tf_op jit(solution)/shard_map/reduce_scatter | solution.py:117
  414.1 37.3 %copy-start.2 = (bf16[1024,256]{1,0:T(8,128)(2,1)S(1)}, bf16[1024,256]{1,0:T(8,128)(2,1)}, u32[]{:S(2)}) copy-start(bf16[1024,256]{1,0:T(8,128)(2,1)} %add_convert_fusion.1) | copy-start | bytes 1572868
Sparse Core Ops, SparseCore 0:
  9.7 38.4 all-gather.6
  50.9 53.7 all-gather.8
  106.8 42.7 all-gather.10
  154.2 78.1 reduce-scatter.2
  234.6 34.9 all-gather.12
  271.5 67.7 all-gather.14
  341.4 57.2 all-gather.16
  414.2 37.1 reduce-scatter.4
